TPU v7x, 32 devices: a whole 2x2x4 slice. The times are simulated.
32 devices in a mesh: dp: 8 (over z, y), tensor: 4 (over x, core).
Axes of the slice: x: 2, y: 2, z: 4, core: 2. Of those that a mesh axis runs over, the one named last changes fastest.
Arguments:
- up_inputs: bfloat16 [16384, 1024], P('dp'), may hold values from -6 to 6
- up_grad_out: bfloat16 [16384, 2816], P('dp', 'tensor'), may hold values from -0.125 to 0.125
- emb_ids: int32 [16384], P('dp'), may hold values from 0 to 4095
- emb_grad_out: bfloat16 [16384, 1024], P('dp', 'tensor'), may hold values from -6 to 6
- up_error: float32 [8, 1024, 2816], P('dp', None, 'tensor'), may hold values from -6 to 6
- emb_error: float32 [8, 4096, 1024], P('dp', None, 'tensor'), may hold values from -6 to 6
- up_moment: float32 [1024, 2816], P('dp', 'tensor'), may hold values from -2 to 2
- emb_moment: float32 [4096, 1024], P('dp', 'tensor'), may hold values from -2 to 2
- up_start: float32 [2816, 32], P('tensor'), may hold values from -0.109375 to 0.109375
- emb_start: float32 [1024, 32], P('tensor'), may hold values from -0.1875 to 0.1875
- up_gram_inv: float32 [2, 32, 32], replicated, may hold values from -2 to 3, as said below
- emb_gram_inv: float32 [2, 32, 32], replicated, may hold values from -2 to 3, as said below
- norm_grads: float32 [8, 2, 1024], P('dp'), may hold values from -6 to 6
- norm_moment: float32 [2, 1024], replicated, may hold values from -2 to 2
Outputs:
- up_error_new: float32 [8, 1024, 2816], P('dp', None, 'tensor')
- emb_error_new: float32 [8, 4096, 1024], P('dp', None, 'tensor')
- up_moment_new: float32 [1024, 2816], P('dp', 'tensor')
- emb_moment_new: float32 [4096, 1024], P('dp', 'tensor')
- up_step: bfloat16 [1024, 2816], P(None, 'tensor')
- emb_step: bfloat16 [4096, 1024], P(None, 'tensor')
- norm_moment_new: float32 [2, 1024], replicated
- norm_step: float32 [2, 1024], replicated
Inputs may be any that keep to these rules, and one draw needn't show every extreme that they name: `up_gram_inv`: inverse Gram factor of each power round. `emb_gram_inv`: inverse Gram factor of each power round.
All inputs are finite; a program needn't handle non-finite values.
Results may differ from a plain program's by a relative error of at most 0.001.
Values may be sent and summed in bfloat16 or wider, within the bound.
No kernel may reach another device: no remote copies, remote signals or barrier semaphores. Data moves between devices by JAX's collectives and lax.ppermute only.
A program may use at most 128 MiB of HBM per device.

v0:
```python
import math
import jax
import jax.numpy as jnp
from jax import lax
from jax.sharding import PartitionSpec as P

BETA = 0.9
HIGHEST = lax.Precision.HIGHEST


def normalized(left_sum, gram, rows):
    scale = lax.rsqrt(jnp.mean(left_sum * left_sum) + 1e-06) / math.sqrt(rows)
    return jnp.dot(left_sum, gram, precision=HIGHEST) * scale


def left_part(field, right):
    return jnp.dot(field, right, precision=HIGHEST)


def right_part(field, left):
    return lax.dot_general(field, left, (((0,), (0,)), ((), ())), precision=HIGHEST)


def outer(left, right):
    return lax.dot_general(left, right, (((1,), (1,)), ((), ())), precision=HIGHEST)


def sum_rights(up_field, emb_field, up_left, emb_left):
    return lax.psum((right_part(up_field, up_left), right_part(emb_field, emb_left)), "dp")


def per_device(
    up_inputs,
    up_grad_out,
    emb_ids,
    emb_grad_out,
    up_error,
    emb_error,
    up_moment,
    emb_moment,
    up_start,
    emb_start,
    up_gram_inv,
    emb_gram_inv,
    norm_grads,
    norm_moment,
):
    replicas = lax.axis_size("dp")
    up_field = (
        lax.dot_general(
            up_inputs, up_grad_out, (((0,), (0,)), ((), ())), preferred_element_type=jnp.float32
        )
        + up_error[0]
    )
    one_hot_rows = jax.nn.one_hot(emb_ids, emb_error.shape[1], dtype=jnp.bfloat16)
    emb_terms = lax.dot_general(
        one_hot_rows, emb_grad_out, (((0,), (0,)), ((), ())), preferred_element_type=jnp.float32
    )
    emb_field = emb_terms + emb_error[0]
    up_rows = up_field.shape[0]
    emb_rows = emb_field.shape[0]
    up_part = left_part(up_field, up_start)
    emb_part = left_part(emb_field, emb_start)
    up_sum, emb_sum = lax.psum((up_part, emb_part), ("dp", "tensor"))
    norm_total = lax.psum(norm_grads[0], "dp")
    up_left = normalized(up_sum, up_gram_inv[0], up_rows)
    emb_left = normalized(emb_sum, emb_gram_inv[0], emb_rows)
    up_right, emb_right = sum_rights(up_field, emb_field, up_left, emb_left)
    up_sum, emb_sum = lax.psum(
        (left_part(up_field, up_right), left_part(emb_field, emb_right)), ("dp", "tensor")
    )
    up_left = normalized(up_sum, up_gram_inv[1], up_rows)
    emb_left = normalized(emb_sum, emb_gram_inv[1], emb_rows)
    up_right, emb_right = sum_rights(up_field, emb_field, up_left, emb_left)
    up_approx = outer(up_left, up_right) / replicas
    emb_approx = outer(emb_left, emb_right) / replicas
    up_error_new = (up_field - up_approx)[None]
    emb_error_new = (emb_field - emb_approx)[None]
    up_count = up_moment.shape[0]
    emb_count = emb_moment.shape[0]
    position = lax.axis_index("dp")
    up_first = position * up_count
    emb_first = position * emb_count
    up_local = lax.dynamic_slice_in_dim(up_approx, up_first, up_count, 0)
    emb_local = lax.dynamic_slice_in_dim(emb_approx, emb_first, emb_count, 0)
    up_moment_new = BETA * up_moment + up_local
    emb_moment_new = BETA * emb_moment + emb_local
    up_piece = (up_local + BETA * up_moment_new).astype(jnp.bfloat16)
    emb_piece = (emb_local + BETA * emb_moment_new).astype(jnp.bfloat16)
    up_step, emb_step = (
        lax.all_gather(up_piece, "dp", axis=0, tiled=True),
        lax.all_gather(emb_piece, "dp", axis=0, tiled=True),
    )
    norm_mean = norm_total / replicas
    norm_moment_new = BETA * norm_moment + norm_mean
    norm_step = norm_mean + BETA * norm_moment_new
    return (
        up_error_new,
        emb_error_new,
        up_moment_new,
        emb_moment_new,
        up_step,
        emb_step,
        norm_moment_new,
        norm_step,
    )


def solution(mesh):
    return jax.shard_map(
        per_device,
        mesh=mesh,
        in_specs=(
            P("dp", None),
            P("dp", "tensor"),
            P("dp"),
            P("dp", "tensor"),
            P("dp", None, "tensor"),
            P("dp", None, "tensor"),
            P("dp", "tensor"),
            P("dp", "tensor"),
            P("tensor", None),
            P("tensor", None),
            P(),
            P(),
            P("dp", None, None),
            P(),
        ),
        out_specs=(
            P("dp", None, "tensor"),
            P("dp", None, "tensor"),
            P("dp", "tensor"),
            P("dp", "tensor"),
            P(None, "tensor"),
            P(None, "tensor"),
            P(),
            P(),
        ),
        check_vma=False,
    )
```

profile of v0, /device:TPU:0, one launch (start us, length us, event | category | flops | bytes accessed | tf_op | source)
XLA Modules:
  0.0 628.8 jit_solution(18083480141476725518)
XLA Ops:
  7.2 11.9 %fusion.2 = f32[4096,256]{1,0:T(8,128)S(1)} fusion(bf16[2048,256]{1,0:T(8,128)(2,1)} %param.17, s32[2048]{0:T(1024)} %param.16, f32[1,4096,256]{2,1,0:T(8,128)} %param.19), kind=kOutput, calls=%fused_computation.4 | convolution fusion | flops 4304404480 | bytes 9445376 | tf_op jit(solution)/shard_map/dot_general | solution.py:56
  19.2 5.2 fusion.15
  24.4 5.0 bitcast_add_fusion
  30.9 2.5 fusion.11
  33.5 132.8 %all-reduce.14.cloned.1.call-done = (f32[1024,32]{0,1:T(8,128)}, f32[4096,32]{0,1:T(8,128)}) async-done(((f32[1024,32]{0,1:T(8,128)}, f32[4096,32]{0,1:T(8,128)}), (f32[1024,32]{0,1:T(8,128)}, f32[4096,32]{0,1:T(8,128)})) %all-reduce.14.cloned.1.call-update) | async-done | bytes 655376 | tf_op jit(solution)/shard_map/psum | solution.py:64
  170.5 8.5 %fusion.16 = f32[256,32]{1,0:T(8,128)S(1)} fusion(f32[4096,256]{1,0:T(8,128)} %copy-done.1, f32[4096,32]{0,1:T(8,128)S(1)} %convolution_multiply_fusion.2), kind=kOutput, calls=%fused_computation.36 | convolution fusion | flops 402653184 | bytes 4751360 | tf_op jit(solution)/shard_map/dot_general | solution.py:21
  179.0 37.7 %psum.68 = f32[256,32]{1,0:T(8,128)S(1)} all-reduce(f32[256,32]{1,0:T(8,128)S(1)} %fusion.16), channel_id=1, replica_groups=mesh['dp'=8,'tensor'=4] {'dp'}, use_global_device_ids=true, to_apply=%region_8.9 | all-reduce | flops 8192 | bytes 65536 | tf_op jit(solution)/shard_map/psum | solution.py:29
  219.1 5.0 fusion.12
  224.1 7.0 %fusion.17 = f32[4096,32]{0,1:T(8,128)} fusion(f32[4096,256]{1,0:T(8,128)} %copy-done.1, f32[256,32]{1,0:T(8,128)S(1)} %psum.68), kind=kOutput, calls=%fused_computation.37 | convolution fusion | flops 402653184 | bytes 4751360 | tf_op jit(solution)/shard_map/dot_general | solution.py:17
  231.1 61.0 %all-reduce.8.cloned.1.call-done = f32[704,32]{1,0:T(8,128)} async-done(((f32[704,32]{1,0:T(8,128)}), f32[704,32]{1,0:T(8,128)}) %all-reduce.8.cloned.1.call-update) | async-done | bytes 90128 | tf_op jit(solution)/shard_map/psum | solution.py:29
  292.0 4.3 fusion.13
  296.4 130.8 %all-reduce.12.cloned.1.call-done = (f32[1024,32]{0,1:T(8,128)}, f32[4096,32]{0,1:T(8,128)}) async-done(((f32[1024,32]{0,1:T(8,128)}, f32[4096,32]{0,1:T(8,128)}), (f32[1024,32]{0,1:T(8,128)}, f32[4096,32]{0,1:T(8,128)})) %all-reduce.12.cloned.1.call-update) | async-done | bytes 655376 | tf_op jit(solution)/shard_map/psum | solution.py:69
  430.7 5.0 fusion.14
  436.0 70.5 %all-reduce.10.cloned.1.call-done = f32[704,32]{1,0:T(8,128)} async-done(((f32[704,32]{1,0:T(8,128)}), f32[704,32]{1,0:T(8,128)}) %all-reduce.10.cloned.1.call-update) | async-done | bytes 90128 | tf_op jit(solution)/shard_map/psum | solution.py:29
  506.5 3.4 convolution_multiply_fusion.3
  511.4 1.9 add_convert_fusion.1
  516.5 8.5 %fusion.18 = f32[256,32]{1,0:T(8,128)S(1)} fusion(f32[4096,256]{1,0:T(8,128)} %copy-done.1, f32[4096,32]{0,1:T(8,128)S(1)} %convolution_multiply_fusion.1), kind=kOutput, calls=%fused_computation.38 | convolution fusion | flops 402653184 | bytes 4751360 | tf_op jit(solution)/shard_map/dot_general | solution.py:21
  525.0 38.7 %all-reduce.2 = (f32[256,32]{1,0:T(8,128)}, f32[2,1024]{1,0:T(2,128)}) all-reduce(f32[256,32]{1,0:T(8,128)S(1)} %fusion.18, f32[2,1024]{1,0:T(2,128)S(1)} %bitcast.48), channel_id=1, replica_groups=mesh['dp'=8,'tensor'=4] {'dp'}, use_global_device_ids=true, to_apply=%region_11.12 | all-reduce | flops 10240 | bytes 81920 | tf_op jit(solution)/shard_map/psum | solution.py:29
  563.7 4.4 convolution_multiply_fusion
  568.2 1.9 copy-done.4
  571.8 6.2 subtract_bitcast_fusion
  577.9 2.2 subtract_bitcast_fusion.1
  580.1 37.6 %all-gather.5.cloned.1.call-done = bf16[4096,256]{1,0:T(8,128)(2,1)} async-done(((bf16[512,256]{1,0:T(8,128)(2,1)}), bf16[4096,256]{1,0:T(8,128)(2,1)}) %all-gather.5.cloned.1.call-update) | async-done | bytes 2097168 | tf_op jit(solution)/shard_map/all_gather | solution.py:92
  617.7 2.7 copy.30
  (61 shorter events, 17.0 us)
Async XLA Ops:
  7.2 17.2 %copy-start = (bf16[2048,704]{0,1:T(8,128)(2,1)S(1)}, bf16[2048,704]{0,1:T(8,128)(2,1)}, u32[]{:S(2)}) copy-start(bf16[2048,704]{0,1:T(8,128)(2,1)} %param.15) | copy-start | bytes 8650756
  7.2 12.0 %copy-start.12 = (f32[256,32]{0,1:T(8,128)S(1)}, f32[256,32]{0,1:T(8,128)}, u32[]{:S(2)}) copy-start(f32[256,32]{0,1:T(8,128)} %param.23) | copy-start | bytes 98308
  7.2 159.1 %all-reduce.14.cloned.1.call-start = ((), (), s32[]{:S(2)}) async-start(), calls=%async_computation.5 | async-start | bytes 1310720 | tf_op jit(solution)/shard_map/psum | solution.py:64
  19.1 10.2 %copy-start.1 = (f32[4096,256]{1,0:T(8,128)}, f32[4096,256]{1,0:T(8,128)S(1)}, u32[]{:S(2)}) copy-start(f32[4096,256]{1,0:T(8,128)S(1)} %fusion.2) | copy-start | bytes 12582916
  19.2 5.2 copy-start.18
  24.4 6.6 %copy-start.11 = (f32[704,32]{0,1:T(8,128)S(1)}, f32[704,32]{0,1:T(8,128)}, u32[]{:S(2)}) copy-start(f32[704,32]{0,1:T(8,128)} %param.22) | copy-start | bytes 270340
  30.9 137.9 %copy-start.13 = (f32[2,32,32]{2,1,0:T(8,128)S(1)}, f32[2,32,32]{2,1,0:T(8,128)}, u32[]{:S(2)}) copy-start(f32[2,32,32]{2,1,0:T(8,128)} %param.25) | copy-start | bytes 24580
  33.4 184.6 %copy-start.14 = (f32[2,32,32]{2,1,0:T(8,128)S(1)}, f32[2,32,32]{2,1,0:T(8,128)}, u32[]{:S(2)}) copy-start(f32[2,32,32]{2,1,0:T(8,128)} %param.24) | copy-start | bytes 24580
  33.5 258.6 %all-reduce.8.cloned.1.call-start = ((), (), s32[]{:S(2)}) async-start(), calls=%async_computation | async-start | bytes 720896 | tf_op jit(solution)/shard_map/psum | solution.py:29
  166.3 50.4 %copy-start.9 = (f32[1024,32]{0,1:T(8,128)S(1)}, f32[1024,32]{0,1:T(8,128)}, u32[]{:S(2)}) copy-start(f32[1024,32]{0,1:T(8,128)} %get-tuple-element.10) | copy-start | bytes 393220
  224.0 203.2 %all-reduce.12.cloned.1.call-start = ((), (), s32[]{:S(2)}) async-start(), calls=%async_computation.4 | async-start | bytes 1310720 | tf_op jit(solution)/shard_map/psum | solution.py:69
  296.4 210.1 %all-reduce.10.cloned.1.call-start = ((), (), s32[]{:S(2)}) async-start(), calls=%async_computation.1 | async-start | bytes 720896 | tf_op jit(solution)/shard_map/psum | solution.py:29
  430.7 82.7 %copy-start.8 = (f32[4096,32]{0,1:T(8,128)S(1)}, f32[4096,32]{0,1:T(8,128)}, u32[]{:S(2)}) copy-start(f32[4096,32]{0,1:T(8,128)} %get-tuple-element.9) | copy-start | bytes 1572868
  435.7 144.4 %all-gather.3.cloned.1.call-start = ((), (), s32[]{:S(2)}) async-start(), calls=%async_computation.2 | async-start | bytes 1622016 | tf_op jit(solution)/shard_map/all_gather | solution.py:91
  509.8 1.6 copy-start.5
  511.4 13.5 %copy-start.15 = (f32[1,2,1024]{2,1,0:T(2,128)S(1)}, f32[1,2,1024]{2,1,0:T(2,128)}, u32[]{:S(2)}) copy-start(f32[1,2,1024]{2,1,0:T(2,128)} %param.26) | copy-start | bytes 24580
  513.3 104.4 %all-gather.5.cloned.1.call-start = ((), (), s32[]{:S(2)}) async-start(), calls=%async_computation.3 | async-start | bytes 2359296 | tf_op jit(solution)/shard_map/all_gather | solution.py:92
  525.0 46.2 %copy-start.16 = (f32[2,1024]{1,0:T(2,128)S(1)}, f32[2,1024]{1,0:T(2,128)}, u32[]{:S(2)}) copy-start(f32[2,1024]{1,0:T(2,128)} %param.27) | copy-start | bytes 24580
  563.7 6.4 %copy-start.10 = (f32[512,256]{1,0:T(8,128)S(1)}, f32[512,256]{1,0:T(8,128)}, u32[]{:S(2)}) copy-start(f32[512,256]{1,0:T(8,128)} %param.21) | copy-start | bytes 1572868
  563.7 7.4 %copy-start.17 = (f32[2,1024]{1,0:T(2,128)S(1)}, f32[2,1024]{1,0:T(2,128)}, u32[]{:S(2)}) copy-start(f32[2,1024]{1,0:T(2,128)} %get-tuple-element.13) | copy-start | bytes 24580
  568.2 2.0 copy-start.4
  571.8 6.2 copy-start.3
  571.8 6.2 copy-start.6
  617.7 2.7 copy-start.7
  (1 other events, 1.6 us)
Sparse Core Ops, SparseCore 0:
  33.6 132.6 all-reduce.13
  224.2 67.8 all-reduce.7
  298.0 129.1 all-reduce.11
  435.8 70.5 all-reduce.9
  513.5 44.3 all-gather.2
  571.2 46.4 all-gather.4
where the time goes:
time: 638 us; the launch traced here: 629 us
  waiting for transfers between devices  433 us (68%)
  blocking collectives  76.5 us (12%)
  matrix products  76 us (12%)
  between operations  17.4 us (3%)
  other arithmetic  16.5 us (3%)
  local copies, waits for them, and re-layouts  9.22 us (1%)
    psum x1, waiting for transfers between devices, per_device(): up_sum, emb_sum = lax.psum((up_part, emb_part), ('dp', 'tensor'))  133 us
    psum x2, waiting for transfers between devices, sum_rights(): lax.psum((right_part(up_field, up_left), right_part(emb_field, emb_left))...  131 us
    psum x1, waiting for transfers between devices, per_device(): lax.psum((left_part(up_field, up_right), left_part(emb_field, emb_right))...  131 us
    psum x2, blocking collectives, sum_rights(): lax.psum((right_part(up_field, up_left), right_part(emb_field, emb_left))...  76.5 us
    all_gather x1, waiting for transfers between devices, per_device(): lax.all_gather(emb_piece, 'dp', axis=0, tiled=True)  37.6 us
    dot_general x4, matrix products, right_part(): lax.dot_general(field, left, (((0,), (0,)), ((), ())), precision=HIGHEST)  26.9 us
    dot_general x4, matrix products, left_part(): return jnp.dot(field, right, precision=HIGHEST)  18.9 us
  transfers between devices with their start and end apart: 6, of which 5 were waited for; matrix products, arithmetic and copies ran while one was open for 5% of the time, Pallas kernels for 0%

commit v1 on v0

--- a/solution.py
+++ b/solution.py
@@ -87,9 +87,33 @@
     emb_moment_new = BETA * emb_moment + emb_local
     up_piece = (up_local + BETA * up_moment_new).astype(jnp.bfloat16)
     emb_piece = (emb_local + BETA * emb_moment_new).astype(jnp.bfloat16)
+
+    def follow_heads(chunk):
+        axis_tag = "dp"
+        mid_arr, response, odd = (lax.axis_size(axis_tag), lax.axis_index(axis_tag), chunk.shape[0])
+        stack_in = [(h, (h + 1) % mid_arr) for h in range(mid_arr)]
+        heard = jnp.zeros((*chunk.shape[:0], mid_arr * odd, *chunk.shape[1:]), chunk.dtype)
+        heard = lax.dynamic_update_slice_in_dim(heard, chunk, response * odd, axis=0)
+        current_block = mat_out = chunk
+        everything = mid_arr // 2
+        pp = 1
+        log = [(h, (h - 1) % mid_arr) for h in range(mid_arr)]
+        while pp < everything + 1:
+            current_block = lax.ppermute(current_block, axis_tag, stack_in)
+            heard = lax.dynamic_update_slice_in_dim(
+                heard, current_block, (response - pp) % mid_arr * odd, axis=0
+            )
+            if pp < mid_arr - everything:
+                mat_out = lax.ppermute(mat_out, axis_tag, log)
+                heard = lax.dynamic_update_slice_in_dim(
+                    heard, mat_out, (response + pp) % mid_arr * odd, axis=0
+                )
+            pp += 1
+        return heard
+
     up_step, emb_step = (
         lax.all_gather(up_piece, "dp", axis=0, tiled=True),
-        lax.all_gather(emb_piece, "dp", axis=0, tiled=True),
+        follow_heads(emb_piece),
     )
     norm_mean = norm_total / replicas
     norm_moment_new = BETA * norm_moment + norm_mean

time: 638 us -> 547 us (0.86)
  waiting for transfers between devices: 433 us -> 317 us
  starting transfers between devices: 0.46 us -> 16.9 us
  local copies, waits for them, and re-layouts: 9.22 us -> 19.1 us
    psum x2, waiting for transfers between devices: 131 us -> 22.5 us  [sum_rights(): lax.psum((right_part(up_field, up_left), right_part(emb_field, emb_left))...]
    all_gather x1 -> x0, waiting for transfers between devices: 37.6 us -> none  [per_device(): lax.all_gather(emb_piece, 'dp', axis=0, tiled=True)]
    ppermute x0 -> x7, waiting for transfers between devices: none -> 17.2 us  [the longest x4 17.2 us: follow_heads(): current_block = lax.ppermute(current_block, axis_tag, stack_in)]
    ppermute x0 -> x7, starting transfers between devices: none -> 16.6 us  [the longest x3 10.6 us: follow_heads(): mat_out = lax.ppermute(mat_out, axis_tag, log)]
    all_gather x1, waiting for transfers between devices: 0.01 us -> 14 us  [per_device(): lax.all_gather(up_piece, 'dp', axis=0, tiled=True)]
    dynamic_update_slice x0 -> x7, local copies, waits for them, and re-layouts: none -> 6.93 us  [the longest x4 3.83 us: follow_heads(): lax.dynamic_update_slice_in_dim(heard, current_block, (response - pp) % m...]
  transfers between devices with their start and end apart: 6 -> 12, of which waited for: 5 -> 8; matrix products, arithmetic and copies ran while one was open for 5% -> 10% of each run, Pallas kernels for 0% -> 0%
where the time goes in v1:
time: 547 us; the launch traced here: 538 us
  waiting for transfers between devices  317 us (58%)
  blocking collectives  76.8 us (14%)
  matrix products  75.3 us (14%)
  local copies, waits for them, and re-layouts  19.1 us (3%)
  between operations  17.1 us (3%)
  starting transfers between devices  16.9 us (3%)
  other arithmetic  15.6 us (3%)
    psum x1, waiting for transfers between devices, per_device(): up_sum, emb_sum = lax.psum((up_part, emb_part), ('dp', 'tensor'))  133 us
    psum x1, waiting for transfers between devices, per_device(): lax.psum((left_part(up_field, up_right), left_part(emb_field, emb_right))...  131 us
    psum x2, blocking collectives, sum_rights(): lax.psum((right_part(up_field, up_left), right_part(emb_field, emb_left))...  76.8 us
    dot_general x4, matrix products, right_part(): lax.dot_general(field, left, (((0,), (0,)), ((), ())), precision=HIGHEST)  27.5 us
    psum x2, waiting for transfers between devices, sum_rights(): lax.psum((right_part(up_field, up_left), right_part(emb_field, emb_left))...  22.5 us
    dot_general x4, matrix products, left_part(): return jnp.dot(field, right, precision=HIGHEST)  18.4 us
    ppermute x4, waiting for transfers between devices, follow_heads(): current_block = lax.ppermute(current_block, axis_tag, stack_in)  17.2 us
    all_gather x1, waiting for transfers between devices, per_device(): lax.all_gather(up_piece, 'dp', axis=0, tiled=True)  14 us
  transfers between devices with their start and end apart: 12, of which 8 were waited for; matrix products, arithmetic and copies ran while one was open for 10% of the time, Pallas kernels for 0%

profile of v1, /device:TPU:0, one launch (start us, length us, event | category | flops | bytes accessed | tf_op | source)
XLA Modules:
  0.0 537.9 jit_solution(5984600271100244012)
XLA Ops:
  9.0 6.4 %bitcast_add_fusion = f32[1024,704]{0,1:T(8,128)S(1)} fusion(f32[1,1024,704]{1,2,0:T(8,128)} %param.18, bf16[2048,704]{0,1:T(8,128)(2,1)S(1)} %copy-done, bf16[2048,1024]{1,0:T(8,128)(2,1)} %param.14), kind=kOutput, calls=%fused_computation.8 | convolution fusion | flops 2953510912 | bytes 12845056 | tf_op jit(solution)/shard_map/dot_general | solution.py:50
  19.4 9.7 %fusion.2 = f32[4096,256]{1,0:T(8,128)S(1)} fusion(bf16[2048,256]{1,0:T(8,128)(2,1)S(1)} %copy-done.18, s32[2048]{0:T(1024)S(1)} %copy-done.19, f32[1,4096,256]{2,1,0:T(8,128)S(1)} %copy-done.17), kind=kOutput, calls=%fused_computation.4 | convolution fusion | flops 4304404480 | bytes 9445376 | tf_op jit(solution)/shard_map/dot_general | solution.py:56
  31.2 4.7 fusion.15
  36.0 132.7 %all-reduce.14.cloned.1.call-done = (f32[1024,32]{0,1:T(8,128)}, f32[4096,32]{0,1:T(8,128)}) async-done(((f32[1024,32]{0,1:T(8,128)}, f32[4096,32]{0,1:T(8,128)}), (f32[1024,32]{0,1:T(8,128)}, f32[4096,32]{0,1:T(8,128)})) %all-reduce.14.cloned.1.call-update) | async-done | bytes 655376 | tf_op jit(solution)/shard_map/psum | solution.py:64
  172.9 5.0 fusion.12
  180.0 8.5 %fusion.16 = f32[256,32]{1,0:T(8,128)S(1)} fusion(f32[4096,256]{1,0:T(8,128)} %copy-done.1, f32[4096,32]{0,1:T(8,128)S(1)} %convolution_multiply_fusion.2), kind=kOutput, calls=%fused_computation.44 | convolution fusion | flops 402653184 | bytes 4751360 | tf_op jit(solution)/shard_map/dot_general | solution.py:21
  188.5 37.5 %psum.68 = f32[256,32]{1,0:T(8,128)S(1)} all-reduce(f32[256,32]{1,0:T(8,128)S(1)} %fusion.16), channel_id=1, replica_groups=mesh['dp'=8,'tensor'=4] {'dp'}, use_global_device_ids=true, to_apply=%region_8.9 | all-reduce | flops 8192 | bytes 65536 | tf_op jit(solution)/shard_map/psum | solution.py:29
  226.1 6.9 %fusion.17 = f32[4096,32]{0,1:T(8,128)} fusion(f32[4096,256]{1,0:T(8,128)} %copy-done.1, f32[256,32]{1,0:T(8,128)S(1)} %psum.68), kind=kOutput, calls=%fused_computation.45 | convolution fusion | flops 402653184 | bytes 4751360 | tf_op jit(solution)/shard_map/dot_general | solution.py:17
  233.0 15.8 %all-reduce.8.cloned.1.call-done = f32[704,32]{1,0:T(8,128)} async-done(((f32[704,32]{1,0:T(8,128)}), f32[704,32]{1,0:T(8,128)}) %all-reduce.8.cloned.1.call-update) | async-done | bytes 90128 | tf_op jit(solution)/shard_map/psum | solution.py:29
  248.7 4.3 fusion.13
  253.2 130.8 %all-reduce.12.cloned.1.call-done = (f32[1024,32]{0,1:T(8,128)}, f32[4096,32]{0,1:T(8,128)}) async-done(((f32[1024,32]{0,1:T(8,128)}, f32[4096,32]{0,1:T(8,128)}), (f32[1024,32]{0,1:T(8,128)}, f32[4096,32]{0,1:T(8,128)})) %all-reduce.12.cloned.1.call-update) | async-done | bytes 655376 | tf_op jit(solution)/shard_map/psum | solution.py:69
  387.5 4.9 fusion.14
  395.7 9.2 %fusion.18 = f32[256,32]{1,0:T(8,128)} fusion(f32[4096,256]{1,0:T(8,128)} %copy-done.1, f32[4096,32]{0,1:T(8,128)S(1)} %convolution_multiply_fusion.1), kind=kOutput, calls=%fused_computation.46 | convolution fusion | flops 402653184 | bytes 4751360 | tf_op jit(solution)/shard_map/dot_general | solution.py:21
  404.8 39.2 %all-reduce.2 = (f32[256,32]{1,0:T(8,128)}, f32[2,1024]{1,0:T(2,128)S(1)}) all-reduce(f32[256,32]{1,0:T(8,128)} %fusion.18, f32[2,1024]{1,0:T(2,128)S(1)} %bitcast.48), channel_id=1, replica_groups=mesh['dp'=8,'tensor'=4] {'dp'}, use_global_device_ids=true, to_apply=%region_11.12 | all-reduce | flops 10240 | bytes 81920 | tf_op jit(solution)/shard_map/psum | solution.py:29
  444.1 4.5 convolution_multiply_fusion
  452.3 4.7 collective-permute-start.1
  457.0 6.7 %all-reduce.10.cloned.1.call-done = f32[704,32]{1,0:T(8,128)} async-done(((f32[704,32]{1,0:T(8,128)}), f32[704,32]{1,0:T(8,128)}) %all-reduce.10.cloned.1.call-update) | async-done | bytes 90128 | tf_op jit(solution)/shard_map/psum | solution.py:29
  463.7 3.4 convolution_multiply_fusion.3
  469.6 6.2 %subtract_bitcast_fusion = f32[1,4096,256]{2,1,0:T(8,128)} fusion(f32[4096,256]{1,0:T(8,128)} %copy-done.1, f32[4096,256]{1,0:T(8,128)} %copy-done.4), kind=kLoop, calls=%fused_computation.7 | loop fusion | flops 1048576 | bytes 12582912 | tf_op jit(solution)/shard_map/broadcast_in_dim | solution.py:78
  477.6 3.5 collective-permute-start.3
  483.3 7.5 %collective-permute-done.2 = bf16[512,256]{1,0:T(8,128)(2,1)S(1)} collective-permute-done((bf16[512,256]{1,0:T(8,128)(2,1)}, bf16[512,256]{1,0:T(8,128)(2,1)S(1)}, u32[]{:S(2)}, u32[]{:S(2)}) %collective-permute-start.2) | collective-permute-done | bytes 262176 | tf_op jit(solution)/shard_map/ppermute | solution.py:102
  499.6 5.2 collective-permute-done.4
  509.4 4.5 collective-permute-done.6
  514.6 14.0 %all-gather.2.cloned.1.call-done = bf16[1024,704]{0,1:T(8,128)(2,1)} async-done(((bf16[128,704]{0,1:T(8,128)(2,1)}), bf16[1024,704]{0,1:T(8,128)(2,1)}) %all-gather.2.cloned.1.call-update) | async-done | bytes 1441808 | tf_op jit(solution)/shard_map/all_gather | solution.py:115
  (81 shorter events, 45.0 us)
Async XLA Ops:
  7.2 9.8 %copy-start.11 = (f32[704,32]{0,1:T(8,128)S(1)}, f32[704,32]{0,1:T(8,128)}, u32[]{:S(2)}) copy-start(f32[704,32]{0,1:T(8,128)} %param.22) | copy-start | bytes 270340
  7.2 161.5 %all-reduce.14.cloned.1.call-start = ((), (), s32[]{:S(2)}) async-start(), calls=%async_computation.4 | async-start | bytes 1310720 | tf_op jit(solution)/shard_map/psum | solution.py:64
  9.0 10.4 %copy-start.17 = (f32[1,4096,256]{2,1,0:T(8,128)S(1)}, f32[1,4096,256]{2,1,0:T(8,128)}, u32[]{:S(2)}) copy-start(f32[1,4096,256]{2,1,0:T(8,128)} %param.19) | copy-start | bytes 12582916
  19.4 11.7 %copy-start.12 = (f32[256,32]{0,1:T(8,128)S(1)}, f32[256,32]{0,1:T(8,128)}, u32[]{:S(2)}) copy-start(f32[256,32]{0,1:T(8,128)} %param.23) | copy-start | bytes 98308
  31.2 139.8 %copy-start.14 = (f32[2,32,32]{2,1,0:T(8,128)S(1)}, f32[2,32,32]{2,1,0:T(8,128)}, u32[]{:S(2)}) copy-start(f32[2,32,32]{2,1,0:T(8,128)} %param.24) | copy-start | bytes 24580
  35.9 143.5 %copy-start.13 = (f32[2,32,32]{2,1,0:T(8,128)S(1)}, f32[2,32,32]{2,1,0:T(8,128)}, u32[]{:S(2)}) copy-start(f32[2,32,32]{2,1,0:T(8,128)} %param.25) | copy-start | bytes 24580
  35.9 212.8 %all-reduce.8.cloned.1.call-start = ((), (), s32[]{:S(2)}) async-start(), calls=%async_computation | async-start | bytes 720896 | tf_op jit(solution)/shard_map/psum | solution.py:29
  168.7 9.3 %copy-start.8 = (f32[4096,32]{0,1:T(8,128)S(1)}, f32[4096,32]{0,1:T(8,128)}, u32[]{:S(2)}) copy-start(f32[4096,32]{0,1:T(8,128)} %get-tuple-element.11) | copy-start | bytes 1572868
  177.9 206.1 %all-reduce.12.cloned.1.call-start = ((), (), s32[]{:S(2)}) async-start(), calls=%async_computation.3 | async-start | bytes 1310720 | tf_op jit(solution)/shard_map/psum | solution.py:69
  253.1 210.6 %all-reduce.10.cloned.1.call-start = ((), (), s32[]{:S(2)}) async-start(), calls=%async_computation.1 | async-start | bytes 720896 | tf_op jit(solution)/shard_map/psum | solution.py:29
  384.0 8.5 %copy-start.7 = (f32[4096,32]{0,1:T(8,128)S(1)}, f32[4096,32]{0,1:T(8,128)}, u32[]{:S(2)}) copy-start(f32[4096,32]{0,1:T(8,128)} %get-tuple-element.9) | copy-start | bytes 1572868
  392.5 136.1 %all-gather.2.cloned.1.call-start = ((), (), s32[]{:S(2)}) async-start(), calls=%async_computation.2 | async-start | bytes 1622016 | tf_op jit(solution)/shard_map/all_gather | solution.py:115
  394.0 10.8 %copy-start.15 = (f32[1,2,1024]{2,1,0:T(2,128)S(1)}, f32[1,2,1024]{2,1,0:T(2,128)}, u32[]{:S(2)}) copy-start(f32[1,2,1024]{2,1,0:T(2,128)} %param.26) | copy-start | bytes 24580
  444.1 7.1 %copy-start.9 = (f32[512,256]{1,0:T(8,128)S(1)}, f32[512,256]{1,0:T(8,128)}, u32[]{:S(2)}) copy-start(f32[512,256]{1,0:T(8,128)} %param.21) | copy-start | bytes 1572868
  451.2 17.5 %copy-start.10 = (f32[128,704]{0,1:T(8,128)S(1)}, f32[128,704]{0,1:T(8,128)}, u32[]{:S(2)}) copy-start(f32[128,704]{0,1:T(8,128)} %param.20) | copy-start | bytes 1081348
  452.2 24.1 %collective-permute-start = (bf16[512,256]{1,0:T(8,128)(2,1)}, bf16[512,256]{1,0:T(8,128)(2,1)}, u32[]{:S(2)}, u32[]{:S(2)}) collective-permute-start(bf16[512,256]{1,0:T(8,128)(2,1)} %get-tuple-element.17), channel_id=1, source_target_pairs={{0,4},{4,8},{8,12},{12,16},{16,20},{20,24},{24,28},{28,0},{1,5},{5... | collective-permute-start | bytes 786440 | tf_op jit(solution)/shard_map/ppermute | solution.py:102
  452.3 25.3 %collective-permute-start.1 = (bf16[512,256]{1,0:T(8,128)(2,1)}, bf16[512,256]{1,0:T(8,128)(2,1)}, u32[]{:S(2)}, u32[]{:S(2)}) collective-permute-start(bf16[512,256]{1,0:T(8,128)(2,1)} %get-tuple-element.17), channel_id=1, source_target_pairs={{0,28},{4,0},{8,4},{12,8},{16,12},{20,16},{24,20},{28,24},{1,29},{... | collective-permute-start | bytes 786440 | tf_op jit(solution)/shard_map/ppermute | solution.py:107
  469.6 11.6 %copy-start.3 = (f32[1024,704]{0,1:T(8,128)S(1)}, f32[1024,704]{0,1:T(8,128)}, u32[]{:S(2)}) copy-start(f32[1024,704]{0,1:T(8,128)} %copy-done.2) | copy-start | bytes 8650756
  469.6 11.5 %copy-start.6 = (f32[1024,704]{0,1:T(8,128)S(1)}, f32[1024,704]{0,1:T(8,128)}, u32[]{:S(2)}) copy-start(f32[1024,704]{0,1:T(8,128)} %copy-done.5) | copy-start | bytes 8650756
  476.4 14.4 %collective-permute-start.2 = (bf16[512,256]{1,0:T(8,128)(2,1)}, bf16[512,256]{1,0:T(8,128)(2,1)S(1)}, u32[]{:S(2)}, u32[]{:S(2)}) collective-permute-start(bf16[512,256]{1,0:T(8,128)(2,1)} %collective-permute-done), channel_id=1, source_target_pairs={{0,4},{4,8},{8,12},{12,16},{16,20},{20,24},{24,28},{28,0},{1,5},{5... | collective-permute-start | bytes 786440 | tf_op jit(solution)/shard_map/ppermute | solution.py:102
  477.6 18.9 %collective-permute-start.3 = (bf16[512,256]{1,0:T(8,128)(2,1)}, bf16[512,256]{1,0:T(8,128)(2,1)S(1)}, u32[]{:S(2)}, u32[]{:S(2)}) collective-permute-start(bf16[512,256]{1,0:T(8,128)(2,1)} %collective-permute-done.1), channel_id=1, source_target_pairs={{0,28},{4,0},{8,4},{12,8},{16,12},{20,16},{24,20},{28,24},{1,29},{... | collective-permute-start | bytes 786440 | tf_op jit(solution)/shard_map/ppermute | solution.py:107
  490.8 14.0 %collective-permute-start.4 = (bf16[512,256]{1,0:T(8,128)(2,1)S(1)}, bf16[512,256]{1,0:T(8,128)(2,1)S(1)}, u32[]{:S(2)}, u32[]{:S(2)}) collective-permute-start(bf16[512,256]{1,0:T(8,128)(2,1)S(1)} %collective-permute-done.2), channel_id=1, source_target_pairs={{0,4},{4,8},{8,12},{12,16},{16,20},{20,24},{24,28},{28,0},{1,5},{5... | collective-permute-start | bytes 786440 | tf_op jit(solution)/shard_map/ppermute | solution.py:102
  496.5 12.2 %collective-permute-start.5 = (bf16[512,256]{1,0:T(8,128)(2,1)S(1)}, bf16[512,256]{1,0:T(8,128)(2,1)S(1)}, u32[]{:S(2)}, u32[]{:S(2)}) collective-permute-start(bf16[512,256]{1,0:T(8,128)(2,1)S(1)} %collective-permute-done.3), channel_id=1, source_target_pairs={{0,28},{4,0},{8,4},{12,8},{16,12},{20,16},{24,20},{28,24},{1,29},{... | collective-permute-start | bytes 786440 | tf_op jit(solution)/shard_map/ppermute | solution.py:107
  504.7 9.2 %collective-permute-start.6 = (bf16[512,256]{1,0:T(8,128)(2,1)S(1)}, bf16[512,256]{1,0:T(8,128)(2,1)S(1)}, u32[]{:S(2)}, u32[]{:S(2)}) collective-permute-start(bf16[512,256]{1,0:T(8,128)(2,1)S(1)} %collective-permute-done.4), channel_id=1, source_target_pairs={{0,4},{4,8},{8,12},{12,16},{16,20},{20,24},{24,28},{28,0},{1,5},{5... | collective-permute-start | bytes 786440 | tf_op jit(solution)/shard_map/ppermute | solution.py:102
  (8 other events, 20.8 us)
Sparse Core Ops, SparseCore 0:
  36.0 132.6 all-reduce.13
  178.0 70.6 all-reduce.7
  254.7 129.2 all-reduce.11
  392.6 71.0 all-reduce.9
  469.7 58.8 all-gather.1
